TPU v7x, 256 devices: a whole 4x4x8 slice. The times are simulated.
256 devices in a mesh: scene: 16 (over y, z_hi), seq: 16 (over z_lo, x, core).
Axes of the slice: x: 4, y: 4, z: 8 (z_hi: 4, z_lo: 2; z = z_hi * 2 + z_lo), core: 2. Of those that a mesh axis runs over, the one named last changes fastest.
Arguments:
- scene_x: bfloat16 [16, 65536, 256], P('scene', 'seq'), may hold values from -6 to 6
- cotangent: bfloat16 [16, 65536, 256], P('scene', 'seq'), may hold values from -6 to 6
- gate_gain: float32 [256], replicated, may hold values from 0.3 to 3
- kernel: bfloat16 [256, 256, 256], P(None, 'seq'), may hold values from -6 to 6
- block_mix: bfloat16 [256, 256], replicated, may hold values from -0.375 to 0.375
- across_mix: bfloat16 [256, 256], replicated, may hold values from -0.375 to 0.375
- across_unmix: bfloat16 [256, 256], replicated, may hold values from -0.375 to 0.375
- block_unmix: bfloat16 [256, 256], replicated, may hold values from -0.375 to 0.375
Outputs:
- mixed: bfloat16 [16, 65536, 256], P('scene', 'seq')
- grad_x: bfloat16 [16, 65536, 256], P('scene', 'seq')
- grad_kernel: float32 [256, 256, 256], P('scene', 'seq')
- grad_gain: float32 [256], replicated
All inputs are finite; a program needn't handle non-finite values.
Results may differ from a plain program's by a relative error of at most 0.007.
Values may be sent and summed in bfloat16 or wider, within the bound.
No kernel may reach another device: no remote copies, remote signals or barrier semaphores. Data moves between devices by JAX's collectives and lax.ppermute only.
A program may use at most 128 MiB of HBM per device.

v0:
```python
import jax
import jax.numpy as jnp
from jax import lax
from jax.sharding import PartitionSpec as P


def on_device(
    scene_x, cotangent, gate_gain, kernel, block_mix, across_mix, across_unmix, block_unmix
):
    f32 = jnp.float32
    bf16 = jnp.bfloat16
    scenes_here, row_count, channels = scene_x.shape
    block_len = block_mix.shape[0]
    local_a = row_count // block_len
    parts = lax.axis_size("seq")
    chunk = block_len // parts
    kernel_f = kernel.astype(f32)
    inputs = scene_x.reshape(scenes_here, local_a, block_len, channels)
    upstream = cotangent.reshape(scenes_here, local_a, block_len, channels).astype(f32)
    gate_pre = inputs.astype(f32) * gate_gain
    gate_sig = jax.nn.sigmoid(gate_pre)
    gate = gate_pre * gate_sig
    grad_values = (upstream * gate).astype(bf16)
    mix_by_dest = block_mix.reshape(parts, chunk, block_len)
    unmix_by_dest = block_unmix.reshape(block_len, parts, chunk)
    first_mix = jnp.einsum(
        "Jjb,sabc->Jsajc", mix_by_dest, inputs, preferred_element_type=f32
    ).astype(bf16)
    grad_unmixed = jnp.einsum(
        "qJj,saqc->Jsajc", unmix_by_dest, grad_values, preferred_element_type=f32
    ).astype(bf16)
    outgoing = jnp.stack([first_mix, grad_unmixed], axis=1)
    incoming = lax.all_to_all(outgoing, "seq", split_axis=0, concat_axis=0, tiled=True)
    incoming = jnp.moveaxis(incoming, 2, 1)
    spread_mix = incoming[:, :, 0].reshape(parts, scenes_here, local_a, chunk, channels)
    spread_grad = incoming[:, :, 1].reshape(parts, scenes_here, local_a, chunk, channels)
    spread_mix = jnp.moveaxis(spread_mix, 1, 0).reshape(
        scenes_here, parts * local_a, chunk, channels
    )
    spread_grad = jnp.moveaxis(spread_grad, 1, 0).reshape(
        scenes_here, parts * local_a, chunk, channels
    )
    second_mix = jnp.einsum(
        "ia,sajc->sijc", across_mix, spread_mix, preferred_element_type=f32
    ).astype(bf16)
    weighted = (second_mix.astype(f32) * kernel_f).astype(bf16)
    unmixed = jnp.einsum(
        "pi,sijc->spjc", across_unmix, weighted, preferred_element_type=f32
    ).astype(bf16)
    grad_weighted = jnp.einsum(
        "pi,spjc->sijc", across_unmix, spread_grad, preferred_element_type=f32
    )
    kernel_term = jnp.sum(grad_weighted * second_mix.astype(f32), axis=0)
    kernel_grad = lax.psum_scatter(kernel_term, "scene", scatter_dimension=0, tiled=True)
    grad_second = (grad_weighted * kernel_f).astype(bf16)
    grad_first = jnp.einsum(
        "ia,sijc->sajc", across_mix, grad_second, preferred_element_type=f32
    ).astype(bf16)
    back = jnp.stack(
        [
            unmixed.reshape(scenes_here, parts, local_a, chunk, channels),
            grad_first.reshape(scenes_here, parts, local_a, chunk, channels),
        ],
        axis=2,
    )
    back = jnp.moveaxis(back, 1, 0)
    returned = lax.all_to_all(back, "seq", split_axis=0, concat_axis=0, tiled=True)
    values = jnp.einsum(
        "qJj,Jsajc->saqc", unmix_by_dest, returned[:, :, 0], preferred_element_type=f32
    )
    mixed_out = (values * gate).astype(bf16).reshape(scenes_here, row_count, channels)
    grad_gate = upstream * values * gate_sig * (1.0 + gate_pre * (1.0 - gate_sig))
    grad_input = (
        jnp.einsum("Jjb,Jsajc->sabc", mix_by_dest, returned[:, :, 1], preferred_element_type=f32)
        + grad_gate * gate_gain
    )
    grad_input = grad_input.astype(bf16).reshape(scenes_here, row_count, channels)
    gain_term = jnp.sum(inputs.astype(f32) * grad_gate, axis=(0, 1, 2))
    gain_total = lax.psum(gain_term, ("scene", "seq"))
    total_rows = scenes_here * lax.axis_size("scene") * local_a * parts * block_len
    grad_scale = 1.0 / jnp.sqrt(jnp.float32(total_rows))
    return (mixed_out, grad_input, kernel_grad, gain_total * grad_scale)


def solution(mesh):
    return jax.shard_map(
        on_device,
        mesh=mesh,
        in_specs=(
            P("scene", "seq", None),
            P("scene", "seq", None),
            P(),
            P(None, "seq", None),
            P(),
            P(),
            P(),
            P(),
        ),
        out_specs=(P("scene", "seq", None), P("scene", "seq", None), P("scene", "seq", None), P()),
        check_vma=False,
    )
```

profile of v0, /device:TPU:1, one launch (start us, length us, event | category | flops | bytes accessed | tf_op | source)
XLA Modules:
  0.0 296.9 jit_solution(17493549479198899965)
XLA Ops:
  7.2 1.0 copy.33
  8.3 2.5 convert_bitcast_fusion.2
  10.7 0.4 copy-done.7
  11.1 1.4 multiply_convert_fusion
  12.5 0.7 convert_bitcast_fusion.1
  13.2 0.4 pad_maximum_fusion
  13.6 2.5 copy.34
  16.1 7.6 %all-to-all-start = ((bf16[16,2,1,16,16,256]{5,4,3,2,1,0:T(8,128)(2,1)}), bf16[16,2,1,16,16,256]{5,4,3,2,1,0:T(8,128)(2,1)}, u32[]{:S(2)}, u32[]{:S(2)}) async-start(bf16[16,2,1,16,16,256]{5,4,3,2,1,0:T(8,128)(2,1)} %copy.34), calls=%async_computation | async-start | bytes 8388608 | tf_op jit(solution)/shard_map/all_to_all | solution.py:33
  23.7 2.7 copy.37
  26.5 50.9 %all-to-all-done = bf16[16,2,1,16,16,256]{5,4,3,2,1,0:T(8,128)(2,1)} async-done(((bf16[16,2,1,16,16,256]{5,4,3,2,1,0:T(8,128)(2,1)}), bf16[16,2,1,16,16,256]{5,4,3,2,1,0:T(8,128)(2,1)}, u32[]{:S(2)}, u32[]{:S(2)}) %all-to-all-start) | async-done | bytes 4194336 | tf_op jit(solution)/shard_map/all_to_all | solution.py:33
  77.4 2.6 copy.70
  80.0 0.3 fusion.36
  80.3 0.6 copy-done.9
  80.9 1.7 fusion.22
  82.6 1.7 fusion.18
  84.3 0.8 fusion.28
  85.1 1.2 copy-done.1
  86.2 0.8 fusion.25
  87.0 1.2 copy.42
  88.2 1.2 copy.43
  89.4 2.3 maximum_bitcast_fusion
  91.7 12.0 %all-to-all-start.1 = ((bf16[16,1,2,16,16,256]{5,4,3,2,1,0:T(8,128)(2,1)}), bf16[16,1,2,16,16,256]{5,4,3,2,1,0:T(8,128)(2,1)}, u32[]{:S(2)}, u32[]{:S(2)}) async-start(bf16[16,1,2,16,16,256]{5,4,3,2,1,0:T(8,128)(2,1)} %maximum_bitcast_fusion), calls=%async_computation.1 | async-start | bytes 8388608 | tf_op jit(solution)/shard_map/all_to_all | solution.py:67
  103.7 4.6 %fusion.4 = f32[256,16,256]{0,2,1:T(8,128)} fusion(f32[16,256,256]{2,1,0:T(8,128)} %copy-done.1, bf16[16,256,256]{2,1,0:T(8,128)(2,1)S(1)} %fusion.22), kind=kLoop, calls=%fused_computation.10 | loop fusion | flops 2097152 | bytes 10485760 | tf_op jit(solution)/shard_map/reduce_sum | solution.py:53
  108.3 5.5 %copy.46 = f32[256,16,256]{2,1,0:T(8,128)} copy(f32[256,16,256]{0,2,1:T(8,128)} %fusion.4) | data formatting | bytes 8388608 | tf_op jit(solution)/shard_map/reduce_sum | solution.py:53
  113.9 73.7 %all-to-all-done.1 = bf16[16,1,2,16,16,256]{5,4,3,2,1,0:T(8,128)(2,1)} async-done(((bf16[16,1,2,16,16,256]{5,4,3,2,1,0:T(8,128)(2,1)}), bf16[16,1,2,16,16,256]{5,4,3,2,1,0:T(8,128)(2,1)}, u32[]{:S(2)}, u32[]{:S(2)}) %all-to-all-start.1) | async-done | bytes 4194336 | tf_op jit(solution)/shard_map/all_to_all | solution.py:67
  187.6 4.1 %fusion.35 = (bf16[16,1,1,16,16,256]{5,4,3,2,1,0:T(8,128)(2,1)}, bf16[16,1,1,16,16,256]{5,4,3,2,1,0:T(8,128)(2,1)S(1)}) fusion(bf16[16,1,2,16,16,256]{5,4,3,2,1,0:T(8,128)(2,1)} %all-to-all-done.1), kind=kLoop, calls=%fused_computation.44 | loop fusion | bytes 8388608 | tf_op jit(solution)/shard_map/slice | solution.py:74
  191.6 3.6 %fusion.7 = (f32[1,16,256,256]{3,2,1,0:T(8,128)S(1)}, bf16[1,16,256,256]{3,2,1,0:T(8,128)(2,1)}) fusion(f32[256]{0:T(256)S(1)} %copy-done.11, bf16[1,4096,256]{2,1,0:T(8,128)(2,1)S(1)} %copy-done.3, bf16[256,16,16,1]{0,2,1,3:T(8,128)(2,1)S(1)} %bitcast.170, bf16[16,1,1,16,16,256]{5,4,3,2,1,0:T(8,128)(2,1)S(1)} %get-tuple-element.15, ...), kind=kOutput, calls=%fused_computation.15 | convolution fusion | flops 552599552 | bytes 12715008 | tf_op jit(solution)/shard_map/qJj,Jsajc->saqc/dot_general | solution.py:68
  195.3 2.0 copy-done.5
  197.2 0.7 multiply_reduce_fusion
  198.0 86.4 %psum.7 = f32[256]{0:T(256)S(1)} all-reduce(f32[256]{0:T(256)S(1)} %multiply_reduce_fusion), channel_id=1, replica_groups=mesh['scene'=16,'seq'=16] {'scene','seq'}, use_global_device_ids=true, to_apply=%region_2.0 | all-reduce | flops 256 | bytes 2048 | tf_op jit(solution)/shard_map/psum | solution.py:79
  284.4 0.6 broadcast_multiply_fusion
  285.0 5.1 %fusion.2 = bf16[1,16,256,256]{3,2,1,0:T(8,128)(2,1)} fusion(f32[1,16,256,256]{3,2,1,0:T(8,128)} %copy-done.5, bf16[16,16,256,1]{2,1,0,3:T(8,128)(2,1)S(1)} %bitcast.158, bf16[16,1,1,16,16,256]{5,4,3,2,1,0:T(8,128)(2,1)} %get-tuple-element.14, f32[256]{0:T(256)S(1)} %copy-done.11), kind=kOutput, calls=%fused_computation.7 | convolution fusion | flops 540016640 | bytes 8520704 | tf_op jit(solution)/shard_map/Jjb,Jsajc->sabc/dot_general | solution.py:74
  (23 shorter events, 0.1 us)
Async XLA Ops:
  7.2 1.1 copy-start
  8.2 2.5 copy-start.2
  8.2 2.8 copy-start.7
  8.3 2.8 copy-start.11
  16.1 7.6 %copy-start.6 = (bf16[256,16,256]{2,1,0:T(8,128)(2,1)S(1)}, bf16[256,16,256]{2,1,0:T(8,128)(2,1)}, u32[]{:S(2)}) copy-start(bf16[256,16,256]{2,1,0:T(8,128)(2,1)} %param.11) | copy-start | bytes 6291460
  16.1 61.2 %all-to-all-start = ((bf16[16,2,1,16,16,256]{5,4,3,2,1,0:T(8,128)(2,1)}), bf16[16,2,1,16,16,256]{5,4,3,2,1,0:T(8,128)(2,1)}, u32[]{:S(2)}, u32[]{:S(2)}) async-start(bf16[16,2,1,16,16,256]{5,4,3,2,1,0:T(8,128)(2,1)} %copy.34), calls=%async_computation | async-start | bytes 8388608 | tf_op jit(solution)/shard_map/all_to_all | solution.py:33
  80.0 0.9 copy-start.9
  80.9 1.7 copy-start.10
  82.6 1.7 copy-start.4
  84.3 1.9 copy-start.1
  91.7 95.9 %all-to-all-start.1 = ((bf16[16,1,2,16,16,256]{5,4,3,2,1,0:T(8,128)(2,1)}), bf16[16,1,2,16,16,256]{5,4,3,2,1,0:T(8,128)(2,1)}, u32[]{:S(2)}, u32[]{:S(2)}) async-start(bf16[16,1,2,16,16,256]{5,4,3,2,1,0:T(8,128)(2,1)} %maximum_bitcast_fusion), calls=%async_computation.1 | async-start | bytes 8388608 | tf_op jit(solution)/shard_map/all_to_all | solution.py:67
  103.7 186.4 %reduce-scatter.2.cloned.1.call-start = ((), (), s32[]{:S(2)}) async-start(), calls=%async_computation.3 | async-start | bytes 4456448 | tf_op jit(solution)/shard_map/reduce_scatter | solution.py:54
  113.8 77.8 %copy-start.3 = (bf16[1,4096,256]{2,1,0:T(8,128)(2,1)S(1)}, bf16[1,4096,256]{2,1,0:T(8,128)(2,1)}, u32[]{:S(2)}) copy-start(bf16[1,4096,256]{2,1,0:T(8,128)(2,1)} %param.8) | copy-start | bytes 6291460
  187.6 4.1 %copy-start.8 = (bf16[1,4096,256]{2,1,0:T(8,128)(2,1)S(1)}, bf16[1,4096,256]{2,1,0:T(8,128)(2,1)}, u32[]{:S(2)}) copy-start(bf16[1,4096,256]{2,1,0:T(8,128)(2,1)} %param.9) | copy-start | bytes 6291460
  195.3 2.0 copy-start.5
Sparse Core Ops, SparseCore 0:
  114.0 102.4 reduce-scatter.1
where the time goes:
time: 297 us
  waiting for transfers between devices  125 us (42%)
  blocking collectives  86.4 us (29%)
  local copies, waits for them, and re-layouts  25.3 us (9%)
  starting transfers between devices  19.6 us (7%)
  matrix products  16.7 us (6%)
  between operations  14.2 us (5%)
  other arithmetic  9.95 us (3%)
    psum x1, blocking collectives, on_device(): gain_total = lax.psum(gain_term, ('scene', 'seq'))  86.4 us
    all_to_all x1, waiting for transfers between devices, on_device(): lax.all_to_all(back, 'seq', split_axis=0, concat_axis=0, tiled=True)  73.7 us
    all_to_all x1, waiting for transfers between devices, on_device(): lax.all_to_all(outgoing, 'seq', split_axis=0, concat_axis=0, tiled=True)  50.9 us
    all_to_all x1, starting transfers between devices, on_device(): lax.all_to_all(back, 'seq', split_axis=0, concat_axis=0, tiled=True)  12 us
    unnamed x26, local copies, waits for them, and re-layouts  7.9 us
    all_to_all x1, starting transfers between devices, on_device(): lax.all_to_all(outgoing, 'seq', split_axis=0, concat_axis=0, tiled=True)  7.6 us
  transfers between devices with their start and end apart: 3, of which 2 were waited for; matrix products, arithmetic and copies ran while one was open for 9% of the time, Pallas kernels for 0%

commit v1 on v0

--- a/solution.py
+++ b/solution.py
@@ -2,6 +2,12 @@
 import jax.numpy as jnp
 from jax import lax
 from jax.sharding import PartitionSpec as P
+
+
+def gather_and_add(x, name):
+    pieces = lax.all_gather(x, name, axis=0, tiled=False)
+    total = pieces.sum(axis=0)
+    return total
 
 
 def on_device(
@@ -76,7 +82,7 @@
     )
     grad_input = grad_input.astype(bf16).reshape(scenes_here, row_count, channels)
     gain_term = jnp.sum(inputs.astype(f32) * grad_gate, axis=(0, 1, 2))
-    gain_total = lax.psum(gain_term, ("scene", "seq"))
+    gain_total = gather_and_add(gain_term, ("scene", "seq"))
     total_rows = scenes_here * lax.axis_size("scene") * local_a * parts * block_len
     grad_scale = 1.0 / jnp.sqrt(jnp.float32(total_rows))
     return (mixed_out, grad_input, kernel_grad, gain_total * grad_scale)

time: 297 us -> 282 us (0.949)
  blocking collectives: 86.4 us -> 71.1 us
    psum x1 -> x0, blocking collectives: 86.4 us -> none  [on_device(): gain_total = lax.psum(gain_term, ('scene', 'seq'))]
    all_gather x0 -> x1, blocking collectives: none -> 71.1 us  [gather_and_add(): pieces = lax.all_gather(x, name, axis=0, tiled=False)]
  transfers between devices with their start and end apart: 3 -> 3, of which waited for: 2 -> 2; matrix products, arithmetic and copies ran while one was open for 9% -> 10% of each run, Pallas kernels for 0% -> 0%
where the time goes in v1:
time: 282 us; the launch traced here: 281 us
  waiting for transfers between devices  125 us (44%)
  blocking collectives  71.1 us (25%)
  local copies, waits for them, and re-layouts  24.6 us (9%)
  starting transfers between devices  19.6 us (7%)
  matrix products  16.7 us (6%)
  between operations  14.2 us (5%)
  other arithmetic  10.2 us (4%)
    all_to_all x1, waiting for transfers between devices, on_device(): lax.all_to_all(back, 'seq', split_axis=0, concat_axis=0, tiled=True)  73.7 us
    all_gather x1, blocking collectives, gather_and_add(): pieces = lax.all_gather(x, name, axis=0, tiled=False)  71.1 us
    all_to_all x1, waiting for transfers between devices, on_device(): lax.all_to_all(outgoing, 'seq', split_axis=0, concat_axis=0, tiled=True)  50.9 us
    all_to_all x1, starting transfers between devices, on_device(): lax.all_to_all(back, 'seq', split_axis=0, concat_axis=0, tiled=True)  12 us
    all_to_all x1, starting transfers between devices, on_device(): lax.all_to_all(outgoing, 'seq', split_axis=0, concat_axis=0, tiled=True)  7.6 us
    unnamed x26, local copies, waits for them, and re-layouts  7.2 us
  transfers between devices with their start and end apart: 3, of which 2 were waited for; matrix products, arithmetic and copies ran while one was open for 10% of the time, Pallas kernels for 0%

profile of v1, /device:TPU:1, one launch (start us, length us, event | category | flops | bytes accessed | tf_op | source)
XLA Modules:
  0.0 281.2 jit_solution(5366517599819968146)
XLA Ops:
  7.2 1.0 copy.33
  8.3 2.5 convert_bitcast_fusion.2
  10.7 0.4 copy-done.7
  11.1 1.4 multiply_convert_fusion
  12.5 0.7 convert_bitcast_fusion.1
  13.2 0.4 pad_maximum_fusion
  13.6 2.5 copy.34
  16.1 7.6 %all-to-all-start = ((bf16[16,2,1,16,16,256]{5,4,3,2,1,0:T(8,128)(2,1)}), bf16[16,2,1,16,16,256]{5,4,3,2,1,0:T(8,128)(2,1)}, u32[]{:S(2)}, u32[]{:S(2)}) async-start(bf16[16,2,1,16,16,256]{5,4,3,2,1,0:T(8,128)(2,1)} %copy.34), calls=%async_computation | async-start | bytes 8388608 | tf_op jit(solution)/shard_map/all_to_all | solution.py:39
  23.7 2.7 copy.37
  26.5 50.9 %all-to-all-done = bf16[16,2,1,16,16,256]{5,4,3,2,1,0:T(8,128)(2,1)} async-done(((bf16[16,2,1,16,16,256]{5,4,3,2,1,0:T(8,128)(2,1)}), bf16[16,2,1,16,16,256]{5,4,3,2,1,0:T(8,128)(2,1)}, u32[]{:S(2)}, u32[]{:S(2)}) %all-to-all-start) | async-done | bytes 4194336 | tf_op jit(solution)/shard_map/all_to_all | solution.py:39
  77.4 2.6 copy.70
  80.0 0.3 fusion.36
  80.3 0.6 copy-done.9
  80.9 1.7 fusion.22
  82.6 1.7 fusion.18
  84.3 0.8 fusion.28
  85.1 1.2 copy-done.1
  86.2 0.8 fusion.25
  87.0 1.2 copy.42
  88.2 1.2 copy.43
  89.4 2.3 maximum_bitcast_fusion
  91.7 12.0 %all-to-all-start.1 = ((bf16[16,1,2,16,16,256]{5,4,3,2,1,0:T(8,128)(2,1)}), bf16[16,1,2,16,16,256]{5,4,3,2,1,0:T(8,128)(2,1)}, u32[]{:S(2)}, u32[]{:S(2)}) async-start(bf16[16,1,2,16,16,256]{5,4,3,2,1,0:T(8,128)(2,1)} %maximum_bitcast_fusion), calls=%async_computation.1 | async-start | bytes 8388608 | tf_op jit(solution)/shard_map/all_to_all | solution.py:73
  103.7 4.6 %fusion.4 = f32[256,16,256]{0,2,1:T(8,128)} fusion(f32[16,256,256]{2,1,0:T(8,128)} %copy-done.1, bf16[16,256,256]{2,1,0:T(8,128)(2,1)S(1)} %fusion.22), kind=kLoop, calls=%fused_computation.10 | loop fusion | flops 2097152 | bytes 10485760 | tf_op jit(solution)/shard_map/reduce_sum | solution.py:59
  108.3 5.5 %copy.46 = f32[256,16,256]{2,1,0:T(8,128)} copy(f32[256,16,256]{0,2,1:T(8,128)} %fusion.4) | data formatting | bytes 8388608 | tf_op jit(solution)/shard_map/reduce_sum | solution.py:59
  113.9 73.7 %all-to-all-done.1 = bf16[16,1,2,16,16,256]{5,4,3,2,1,0:T(8,128)(2,1)} async-done(((bf16[16,1,2,16,16,256]{5,4,3,2,1,0:T(8,128)(2,1)}), bf16[16,1,2,16,16,256]{5,4,3,2,1,0:T(8,128)(2,1)}, u32[]{:S(2)}, u32[]{:S(2)}) %all-to-all-start.1) | async-done | bytes 4194336 | tf_op jit(solution)/shard_map/all_to_all | solution.py:73
  187.6 4.1 %fusion.35 = (bf16[16,1,1,16,16,256]{5,4,3,2,1,0:T(8,128)(2,1)}, bf16[16,1,1,16,16,256]{5,4,3,2,1,0:T(8,128)(2,1)S(1)}) fusion(bf16[16,1,2,16,16,256]{5,4,3,2,1,0:T(8,128)(2,1)} %all-to-all-done.1), kind=kLoop, calls=%fused_computation.44 | loop fusion | bytes 8388608 | tf_op jit(solution)/shard_map/slice | solution.py:80
  191.6 3.6 %fusion.7 = (f32[1,16,256,256]{3,2,1,0:T(8,128)S(1)}, bf16[1,16,256,256]{3,2,1,0:T(8,128)(2,1)}) fusion(f32[256]{0:T(256)S(1)} %copy-done.11, bf16[1,4096,256]{2,1,0:T(8,128)(2,1)S(1)} %copy-done.3, bf16[256,16,16,1]{0,2,1,3:T(8,128)(2,1)S(1)} %bitcast.171, bf16[16,1,1,16,16,256]{5,4,3,2,1,0:T(8,128)(2,1)S(1)} %get-tuple-element.15, ...), kind=kOutput, calls=%fused_computation.15 | convolution fusion | flops 552599552 | bytes 12715008 | tf_op jit(solution)/shard_map/qJj,Jsajc->saqc/dot_general | solution.py:74
  195.3 0.7 multiply_reduce_fusion
  196.0 1.3 copy-done.5
  197.2 71.1 %all-gather.1 = f32[256,1,256]{2,1,0:T(1,128)S(1)} all-gather(f32[1,1,256]{2,1,0:T(1,128)S(1)} %bitcast.172), channel_id=2, replica_groups=mesh['scene'=16,'seq'=16] {'scene','seq'}, dimensions={0}, use_global_device_ids=true | all-gather | bytes 263168 | tf_op jit(solution)/shard_map/all_gather | solution.py:8
  268.7 0.6 broadcast_multiply_fusion
  269.2 5.1 %fusion.2 = bf16[1,16,256,256]{3,2,1,0:T(8,128)(2,1)} fusion(f32[1,16,256,256]{3,2,1,0:T(8,128)} %copy-done.5, bf16[16,16,256,1]{2,1,0,3:T(8,128)(2,1)S(1)} %bitcast.159, bf16[16,1,1,16,16,256]{5,4,3,2,1,0:T(8,128)(2,1)} %get-tuple-element.14, f32[256]{0:T(256)S(1)} %copy-done.11), kind=kOutput, calls=%fused_computation.7 | convolution fusion | flops 540016640 | bytes 8520704 | tf_op jit(solution)/shard_map/Jjb,Jsajc->sabc/dot_general | solution.py:80
  (24 shorter events, 0.4 us)
Async XLA Ops:
  7.2 1.1 copy-start
  8.2 2.5 copy-start.2
  8.2 2.8 %copy-start.7 = (bf16[1,4096,256]{2,1,0:T(8,128)(2,1)S(1)}, bf16[1,4096,256]{2,1,0:T(8,128)(2,1)}, u32[]{:S(2)}) copy-start(bf16[1,4096,256]{2,1,0:T(8,128)(2,1)} %param.9) | copy-start | bytes 6291460
  8.3 2.8 %copy-start.11 = (f32[256]{0:T(256)S(1)}, f32[256]{0:T(256)}, u32[]{:S(2)}) copy-start(f32[256]{0:T(256)} %param.10) | copy-start | bytes 3076
  16.1 7.6 %copy-start.6 = (bf16[256,16,256]{2,1,0:T(8,128)(2,1)S(1)}, bf16[256,16,256]{2,1,0:T(8,128)(2,1)}, u32[]{:S(2)}) copy-start(bf16[256,16,256]{2,1,0:T(8,128)(2,1)} %param.11) | copy-start | bytes 6291460
  16.1 61.2 %all-to-all-start = ((bf16[16,2,1,16,16,256]{5,4,3,2,1,0:T(8,128)(2,1)}), bf16[16,2,1,16,16,256]{5,4,3,2,1,0:T(8,128)(2,1)}, u32[]{:S(2)}, u32[]{:S(2)}) async-start(bf16[16,2,1,16,16,256]{5,4,3,2,1,0:T(8,128)(2,1)} %copy.34), calls=%async_computation | async-start | bytes 8388608 | tf_op jit(solution)/shard_map/all_to_all | solution.py:39
  80.0 0.9 copy-start.9
  80.9 1.7 copy-start.10
  82.6 1.7 copy-start.4
  84.3 1.9 copy-start.1
  91.7 95.9 %all-to-all-start.1 = ((bf16[16,1,2,16,16,256]{5,4,3,2,1,0:T(8,128)(2,1)}), bf16[16,1,2,16,16,256]{5,4,3,2,1,0:T(8,128)(2,1)}, u32[]{:S(2)}, u32[]{:S(2)}) async-start(bf16[16,1,2,16,16,256]{5,4,3,2,1,0:T(8,128)(2,1)} %maximum_bitcast_fusion), calls=%async_computation.1 | async-start | bytes 8388608 | tf_op jit(solution)/shard_map/all_to_all | solution.py:73
  103.7 170.6 %reduce-scatter.2.cloned.1.call-start = ((), (), s32[]{:S(2)}) async-start(), calls=%async_computation.3 | async-start | bytes 4456448 | tf_op jit(solution)/shard_map/reduce_scatter | solution.py:60
  113.8 77.8 %copy-start.3 = (bf16[1,4096,256]{2,1,0:T(8,128)(2,1)S(1)}, bf16[1,4096,256]{2,1,0:T(8,128)(2,1)}, u32[]{:S(2)}) copy-start(bf16[1,4096,256]{2,1,0:T(8,128)(2,1)} %param.8) | copy-start | bytes 6291460
  187.6 4.1 %copy-start.8 = (bf16[1,4096,256]{2,1,0:T(8,128)(2,1)S(1)}, bf16[1,4096,256]{2,1,0:T(8,128)(2,1)}, u32[]{:S(2)}) copy-start(bf16[1,4096,256]{2,1,0:T(8,128)(2,1)} %param.9) | copy-start | bytes 6291460
  195.3 2.0 copy-start.5
Sparse Core Ops, SparseCore 0:
  114.0 102.4 reduce-scatter.1
